TPU v7x, 512 devices: a whole 4x4x16 slice. The times are simulated.
512 devices in a mesh: tm: 16 (over z_hi, y), space: 32 (over z_lo, x, core).
Axes of the slice: x: 4, y: 4, z: 16 (z_hi: 4, z_lo: 4; z = z_hi * 4 + z_lo), core: 2. Of those that a mesh axis runs over, the one named last changes fastest.
Arguments:
- queries: bfloat16 [128, 2048, 256], P('tm', 'space'), as said below
- keys: bfloat16 [128, 2048, 256], P('tm', 'space'), as said below
- label_values: bfloat16 [128, 2048, 64], P('tm', 'space'), may hold values from -6 to 6
- class_ids: int32 [128, 2048], P(None, 'space'), may hold values from 0 to 63
- valid_pixels: int32 [128], replicated, may hold values from 1024 to 2048
- keyframe_index: int32 [2, 2], replicated, may hold values from 0 to 127, as said below
Outputs:
- readout: bfloat16 [128, 2048, 64], P('tm', 'space')
- confidence: float32 [2, 2, 2048], P(None, None, 'space')
Inputs may be any that keep to these rules, and one draw needn't show every extreme that they name: `queries`: queries and keys are real-valued embeddings. `keys`: Real-valued embeddings. `keyframe_index`: all 4 entries are different frames.
All inputs are finite; a program needn't handle non-finite values.
Results may differ from a plain program's by a relative error of at most 0.0053.
Values may be sent and summed in bfloat16 or wider, within the bound.
No kernel may reach another device: no remote copies, remote signals or barrier semaphores. Data moves between devices by JAX's collectives and lax.ppermute only.
A program may use at most 192 MiB of HBM per device.

v0:
```python
import math
import jax
import jax.numpy as jnp
from jax import lax
from jax.sharding import PartitionSpec as P

LOWEST = -1e30


def broadcast_tm(values, owners, axis):
    size = lax.axis_size(axis)
    me = lax.axis_index(axis)
    rounds = size.bit_length() - 1
    assert 1 << rounds == size
    for r in range(rounds):
        bit = 1 << r
        pairs = [(i, i ^ bit) for i in range(size)]
        received = lax.ppermute(values, axis, pairs)
        out = []
        for value, owner, got in zip(values, owners, received):
            take = (me ^ owner) >> r == 1
            take = take.reshape(take.shape + (1,) * (value.ndim - take.ndim))
            out.append(jnp.where(take, got, value))
        values = tuple(out)
    return values


def merge_stats(col_max, col_total, col_num, axis):
    top = jnp.max(col_max, axis=axis, keepdims=True)
    keep = jnp.exp(col_max - top)
    total = jnp.sum(col_total * keep, axis=axis)
    num = jnp.sum(col_num * keep, axis=axis)
    return (jnp.squeeze(top, axis), total, num)


def body(queries, keys, label_values, class_ids, valid_pixels, keyframe_index):
    fr_dev, pix_dev, width = queries.shape
    channels = label_values.shape[2]
    total_steps, keyframes = keyframe_index.shape
    n_space = lax.axis_size("space")
    pix_all = pix_dev * n_space
    mem_width = keyframes * pix_all
    time_pos = lax.axis_index("tm")
    space_pos = lax.axis_index("space")
    rows = fr_dev * pix_dev
    scale = 3.0 / math.sqrt(width)
    class_range = jnp.arange(channels, dtype=jnp.int32)
    frame_valid = lax.dynamic_slice_in_dim(valid_pixels, time_pos * fr_dev, fr_dev)
    pixel_ids = space_pos * pix_dev + jnp.arange(pix_dev, dtype=jnp.int32)
    row_valid = (pixel_ids[None, :] < frame_valid[:, None]).reshape(rows)
    query_rows = queries.reshape(rows, width)
    flat_kf = keyframe_index.reshape(-1)
    owners = flat_kf // fr_dev
    slots = flat_kf % fr_dev
    later = keyframes * (total_steps - 1)
    kf_keys = jnp.take(keys, slots, axis=0)
    kf_values = jnp.take(label_values, slots[:keyframes], axis=0)
    kf_queries = jnp.take(queries, slots[keyframes:], axis=0)
    kf_keys, kf_values, kf_queries = broadcast_tm(
        (kf_keys, kf_values, kf_queries), (owners, owners[:keyframes], owners[keyframes:]), "tm"
    )
    kf_ids = jnp.take(class_ids, flat_kf, axis=0).astype(jnp.bfloat16)
    kf_ids = kf_ids.reshape(total_steps, keyframes, pix_dev).transpose(1, 2, 0)
    step_keys = kf_keys.reshape(total_steps, keyframes, pix_dev, width)
    packed = jnp.concatenate(
        [step_keys[s] for s in range(total_steps)] + [kf_values, kf_ids], axis=2
    )
    gathered = lax.all_gather(packed, "space", axis=1, tiled=True)
    mem_keys = [
        gathered[:, :, s * width : (s + 1) * width].reshape(mem_width, width)
        for s in range(total_steps)
    ]
    base = total_steps * width
    mem_values = gathered[:, :, base : base + channels].reshape(mem_width, channels)
    mem_ids = [
        gathered[:, :, base + channels + s].reshape(mem_width).astype(jnp.int32)
        for s in range(total_steps)
    ]
    extra_queries = kf_queries.reshape(later, pix_dev, width)
    extra_valid = pixel_ids[None, :] < jnp.take(valid_pixels, flat_kf[keyframes:])[:, None]
    stats = []
    readout = None
    for step in range(total_steps):
        chosen = keyframe_index[step]
        key_valid = (
            jnp.arange(pix_all, dtype=jnp.int32)[None, :] < jnp.take(valid_pixels, chosen)[:, None]
        ).reshape(mem_width)
        ids = mem_ids[step]
        onehot_t = (ids[None, :] == class_range[:, None]).astype(jnp.bfloat16)
        if step + 1 < total_steps:
            extra = extra_queries[step * keyframes : (step + 1) * keyframes].reshape(-1, width)
            extra_ok = extra_valid[step * keyframes : (step + 1) * keyframes].reshape(-1)
            q = jnp.concatenate([query_rows, extra], axis=0)
            q_valid = jnp.concatenate([row_valid, extra_ok], axis=0)
        else:
            q = query_rows
            q_valid = row_valid
        scores = (
            lax.dot_general(
                q, mem_keys[step], (((1,), (1,)), ((), ())), preferred_element_type=jnp.float32
            )
            * scale
        )
        masked = jnp.where(key_valid[None, :], scores, LOWEST)
        row_max = jnp.max(masked, axis=1, keepdims=True)
        weights = jnp.where(key_valid[None, :], jnp.exp(scores - row_max), 0.0)
        total = jnp.sum(weights, axis=1, keepdims=True)
        mixed = (
            jnp.dot(weights.astype(jnp.bfloat16), mem_values, preferred_element_type=jnp.float32)
            / total
        )
        out = jnp.where(q_valid[:, None], mixed, 0.0).astype(jnp.bfloat16)
        readout = out[:rows]
        own_scores = scores[:rows]
        picked = jnp.dot(readout, onehot_t, preferred_element_type=jnp.float32)
        col_max = jnp.max(jnp.where(row_valid[:, None], own_scores, LOWEST), axis=0)
        expo = jnp.where(row_valid[:, None], jnp.exp(own_scores - col_max[None, :]), 0.0)
        col_total = jnp.sum(expo, axis=0)
        col_num = jnp.sum(expo * picked, axis=0)
        stats.append(jnp.stack([col_max, col_total, col_num]))
        if step + 1 < total_steps:
            part = out[rows:].reshape(keyframes, pix_dev, channels)
            mem_values = lax.all_gather(part, "space", axis=1, tiled=True).reshape(
                mem_width, channels
            )
    local = jnp.stack(stats).reshape(total_steps, 3, keyframes, n_space, pix_dev)
    local = local.transpose(3, 1, 0, 2, 4)
    spread = lax.all_to_all(local, "space", 0, 0, tiled=True)
    m, t, n = merge_stats(spread[:, 0], spread[:, 1], spread[:, 2], 0)
    joined = lax.all_gather(jnp.stack([m, t, n]), "tm", axis=0, tiled=False)
    m, col_total, col_num = merge_stats(joined[:, 0], joined[:, 1], joined[:, 2], 0)
    confidences = []
    for step in range(total_steps):
        chosen = keyframe_index[step]
        key_valid = (
            jnp.arange(pix_all, dtype=jnp.int32)[None, :] < jnp.take(valid_pixels, chosen)[:, None]
        ).reshape(mem_width)
        class_match = mem_ids[step][None, :] == class_range[:, None]
        hits = (class_match & key_valid[None, :]).astype(jnp.int32)
        counts = jnp.sum(hits, axis=1)
        all_count = jnp.sum(counts)
        own_ids = lax.dynamic_slice_in_dim(
            mem_ids[step].reshape(keyframes, pix_all), space_pos * pix_dev, pix_dev, 1
        )
        own_valid = pixel_ids[None, :] < jnp.take(valid_pixels, chosen)[:, None]
        own = jnp.take(counts, own_ids)
        own_safe = jnp.where(own_valid, own, 1)
        factor = jnp.sqrt(all_count.astype(jnp.float32) / (channels * own_safe.astype(jnp.float32)))
        conf = jnp.where(own_valid, col_num[step] / col_total[step] * factor, 0.0)
        confidences.append(conf)
    return (readout.reshape(fr_dev, pix_dev, channels), jnp.stack(confidences))


def solution(mesh):
    placed = (
        P("tm", "space", None),
        P("tm", "space", None),
        P("tm", "space", None),
        P(None, "space"),
        P(),
        P(),
    )
    return jax.shard_map(
        body,
        mesh=mesh,
        in_specs=placed,
        out_specs=(P("tm", "space", None), P(None, None, "space")),
        check_vma=False,
    )
```

profile of v0, /device:TPU:2, one launch (start us, length us, event | category | flops | bytes accessed | tf_op | source)
XLA Modules:
  0.0 316.3 jit_solution(2012742104391452579)
XLA Ops:
  9.5 3.5 %collective-permute-start = (bf16[4,64,256]{2,1,0:T(8,128)(2,1)S(1)}, bf16[4,64,256]{2,1,0:T(8,128)(2,1)S(1)}, u32[]{:S(2)}, u32[]{:S(2)}) collective-permute-start(bf16[4,64,256]{2,1,0:T(8,128)(2,1)S(1)} %broadcast_select_fusion), channel_id=1, source_target_pairs={{0,32},{32,0},{64,96},{96,64},{128,160},{160,128},{192,224},{224,1... | collective-permute-start | bytes 393224 | tf_op jit(solution)/shard_map/ppermute | solution.py:18
  14.6 2.3 collective-permute-start.4
  20.5 4.8 %collective-permute-start.5 = (bf16[2,64,64]{2,1,0:T(8,128)(2,1)S(1)}, bf16[2,64,64]{2,1,0:T(8,128)(2,1)S(1)}, u32[]{:S(2)}, u32[]{:S(2)}) collective-permute-start(bf16[2,64,64]{2,1,0:T(8,128)(2,1)S(1)} %broadcast_select_fusion.11), channel_id=1, source_target_pairs={{0,64},{32,96},{64,0},{96,32},{128,192},{160,224},{192,128},{224,1... | collective-permute-start | bytes 49160 | tf_op jit(solution)/shard_map/ppermute | solution.py:18
  25.4 2.5 collective-permute-start.1
  28.1 9.1 %collective-permute-start.6 = (bf16[2,64,64]{2,1,0:T(8,128)(2,1)S(1)}, bf16[2,64,64]{2,1,0:T(8,128)(2,1)S(1)}, u32[]{:S(2)}, u32[]{:S(2)}) collective-permute-start(bf16[2,64,64]{2,1,0:T(8,128)(2,1)S(1)} %broadcast_select_fusion.12), channel_id=1, source_target_pairs={{0,128},{32,160},{64,192},{96,224},{128,0},{160,32},{192,64},{224,... | collective-permute-start | bytes 49160 | tf_op jit(solution)/shard_map/ppermute | solution.py:18
  37.2 5.7 %collective-permute-start.2 = (bf16[4,64,256]{2,1,0:T(8,128)(2,1)S(1)}, bf16[4,64,256]{2,1,0:T(8,128)(2,1)S(1)}, u32[]{:S(2)}, u32[]{:S(2)}) collective-permute-start(bf16[4,64,256]{2,1,0:T(8,128)(2,1)S(1)} %broadcast_select_fusion.2), channel_id=1, source_target_pairs={{0,128},{32,160},{64,192},{96,224},{128,0},{160,32},{192,64},{224,... | collective-permute-start | bytes 393224 | tf_op jit(solution)/shard_map/ppermute | solution.py:18
  43.1 10.9 %collective-permute-start.7 = (bf16[2,64,64]{2,1,0:T(8,128)(2,1)S(1)}, bf16[2,64,64]{2,1,0:T(8,128)(2,1)S(1)}, u32[]{:S(2)}, u32[]{:S(2)}) collective-permute-start(bf16[2,64,64]{2,1,0:T(8,128)(2,1)S(1)} %broadcast_select_fusion.13), channel_id=1, source_target_pairs={{0,256},{32,288},{64,320},{96,352},{128,384},{160,416},{192,448},{... | collective-permute-start | bytes 49160 | tf_op jit(solution)/shard_map/ppermute | solution.py:18
  54.6 14.0 %collective-permute-start.3 = (bf16[4,64,256]{2,1,0:T(8,128)(2,1)S(1)}, bf16[4,64,256]{2,1,0:T(8,128)(2,1)S(1)}, u32[]{:S(2)}, u32[]{:S(2)}) collective-permute-start(bf16[4,64,256]{2,1,0:T(8,128)(2,1)S(1)} %broadcast_select_fusion.3), channel_id=1, source_target_pairs={{0,256},{32,288},{64,320},{96,352},{128,384},{160,416},{192,448},{... | collective-permute-start | bytes 393224 | tf_op jit(solution)/shard_map/ppermute | solution.py:18
  68.8 11.4 %collective-permute-done.3 = bf16[4,64,256]{2,1,0:T(8,128)(2,1)S(1)} collective-permute-done((bf16[4,64,256]{2,1,0:T(8,128)(2,1)S(1)}, bf16[4,64,256]{2,1,0:T(8,128)(2,1)S(1)}, u32[]{:S(2)}, u32[]{:S(2)}) %collective-permute-start.3) | collective-permute-done | bytes 131104 | tf_op jit(solution)/shard_map/ppermute | solution.py:18
  82.6 2.1 collective-permute-start.8
  89.9 4.3 %collective-permute-start.9 = (bf16[2,64,256]{2,1,0:T(8,128)(2,1)S(1)}, bf16[2,64,256]{2,1,0:T(8,128)(2,1)S(1)}, u32[]{:S(2)}, u32[]{:S(2)}) collective-permute-start(bf16[2,64,256]{2,1,0:T(8,128)(2,1)S(1)} %broadcast_select_fusion.6), channel_id=1, source_target_pairs={{0,64},{32,96},{64,0},{96,32},{128,192},{160,224},{192,128},{224,1... | collective-permute-start | bytes 196616 | tf_op jit(solution)/shard_map/ppermute | solution.py:18
  94.3 3.3 %collective-permute-done.9 = bf16[2,64,256]{2,1,0:T(8,128)(2,1)S(1)} collective-permute-done((bf16[2,64,256]{2,1,0:T(8,128)(2,1)S(1)}, bf16[2,64,256]{2,1,0:T(8,128)(2,1)S(1)}, u32[]{:S(2)}, u32[]{:S(2)}) %collective-permute-start.9) | collective-permute-done | bytes 65568 | tf_op jit(solution)/shard_map/ppermute | solution.py:18
  97.6 1.9 collective-permute-start.10
  99.8 9.3 %collective-permute-done.10 = bf16[2,64,256]{2,1,0:T(8,128)(2,1)S(1)} collective-permute-done((bf16[2,64,256]{2,1,0:T(8,128)(2,1)S(1)}, bf16[2,64,256]{2,1,0:T(8,128)(2,1)S(1)}, u32[]{:S(2)}, u32[]{:S(2)}) %collective-permute-start.10) | collective-permute-done | bytes 65568 | tf_op jit(solution)/shard_map/ppermute | solution.py:18
  109.2 6.2 %collective-permute-start.11 = (bf16[2,64,256]{2,1,0:T(8,128)(2,1)S(1)}, bf16[2,64,256]{2,1,0:T(8,128)(2,1)S(1)}, u32[]{:S(2)}, u32[]{:S(2)}) collective-permute-start(bf16[2,64,256]{2,1,0:T(8,128)(2,1)S(1)} %broadcast_select_fusion.8), channel_id=1, source_target_pairs={{0,256},{32,288},{64,320},{96,352},{128,384},{160,416},{192,448},{... | collective-permute-start | bytes 196616 | tf_op jit(solution)/shard_map/ppermute | solution.py:18
  115.4 10.2 %collective-permute-done.11 = bf16[2,64,256]{2,1,0:T(8,128)(2,1)S(1)} collective-permute-done((bf16[2,64,256]{2,1,0:T(8,128)(2,1)S(1)}, bf16[2,64,256]{2,1,0:T(8,128)(2,1)S(1)}, u32[]{:S(2)}, u32[]{:S(2)}) %collective-permute-start.11) | collective-permute-done | bytes 65568 | tf_op jit(solution)/shard_map/ppermute | solution.py:18
  125.7 23.9 %all-gather.3.cloned.1.call-done = bf16[2,2048,578]{2,1,0:T(8,128)(2,1)} async-done(((bf16[2,64,578]{2,1,0:T(8,128)(2,1)}), bf16[2,2048,578]{2,1,0:T(8,128)(2,1)}) %all-gather.3.cloned.1.call-update) | async-done | bytes 4734992 | tf_op jit(solution)/shard_map/all_gather | solution.py:68
  149.7 3.8 %fusion.62 = (bf16[2,2048,256]{2,1,0:T(8,128)(2,1)}, bf16[2,2048,256]{2,1,0:T(8,128)(2,1)S(1)}) fusion(bf16[2,2048,578]{2,1,0:T(8,128)(2,1)} %all-gather.3.cloned.1.call-done), kind=kLoop, calls=%fused_computation.167 | loop fusion | bytes 8388608 | tf_op jit(solution)/shard_map/slice | solution.py:70
  153.5 1.8 select_reduce_fusion
  156.7 2.6 copy-done.1
  159.3 1.8 fusion.6
  161.2 6.1 %fusion = f32[640]{0:T(1024)S(1)} fusion(f32[640,4096]{1,0:T(8,128)} %copy-done.1, f32[640]{0:T(1024)S(1)} %get-tuple-element.70, pred[4096]{0:T(1024)(128)(4,1)S(1)} %lt.185), kind=kLoop, calls=%fused_computation.10 | loop fusion | flops 7863680 | bytes 10494976 | tf_op jit(solution)/shard_map/reduce_sum | solution.py:107
  167.3 3.4 %fusion.35 = (s32[2,2048]{1,0:T(2,128)S(1)}, s32[2,2048]{1,0:T(2,128)S(1)}) fusion(bf16[2,2048,578]{2,1,0:T(8,128)(2,1)} %all-gather.3.cloned.1.call-done), kind=kLoop, calls=%fused_computation.49 | loop fusion | flops 8192 | bytes 49152 | tf_op jit(solution)/shard_map/convert_element_type | solution.py:76
  170.8 1.9 fusion.28
  172.7 2.7 multiply_reduce_fusion
  176.8 43.1 %all_gather.13 = bf16[2,2048,64]{2,0,1:T(2,128)(2,1)S(1)} all-gather(bf16[2,64,64]{2,0,1:T(2,128)(2,1)S(1)} %copy.47), channel_id=1, replica_groups=mesh['tm'=16,'space'=32] {'space'}, dimensions={1}, use_global_device_ids=true | all-gather | bytes 540672 | tf_op jit(solution)/shard_map/all_gather | solution.py:123
  220.9 6.1 %select_reduce_fusion.1 = (f32[4096]{0:T(1024)S(1)}, f32[512]{0:T(512)S(1)}, f32[4096,512]{0,1:T(8,128)}) fusion(pred[512]{0:T(512)(128)(4,1)S(1)} %lt.168, pred[4096]{0:T(1024)(128)(4,1)S(1)} %lt.172, bf16[4096,256]{1,0:T(8,128)(2,1)} %bitcast.117, bf16[512,256]{1,0:T(8,128)(2,1)S(1)} %bitcast.135), kind=kOutput, calls=%fused_computation.15 | convolution fusion | flops 1084222976 | bytes 10770944 | tf_op jit(solution)/shard_map/dot_general | solution.py:99
  227.0 6.4 %fusion.5 = (f32[4096]{0:T(1024)S(1)}, f32[512]{0:T(512)S(1)}) fusion(f32[4096,512]{0,1:T(8,128)} %get-tuple-element.72, f32[4096]{0:T(1024)S(1)} %get-tuple-element.16, pred[512]{0:T(512)(128)(4,1)S(1)} %lt.168, f32[512]{0:T(512)S(1)} %get-tuple-element.17, pred[4096]{0:T(1024)(128)(4,1)S(1)} %lt.172), kind=kLoop, calls=%fused_computation.24 | loop fusion | flops 12578304 | bytes 8430080 | tf_op jit(solution)/shard_map/reduce_sum | solution.py:118
  235.8 4.7 %fusion.2 = f32[4096]{0:T(1024)S(1)} fusion(f32[4096,512]{0,1:T(8,128)} %get-tuple-element.72, bf16[512,64]{0,1:T(8,128)(2,1)S(1)} %fusion.19, f32[4096]{0:T(1024)S(1)} %get-tuple-element.16, pred[512]{0:T(512)(128)(4,1)S(1)} %lt.168, s32[4096]{0:T(1024)S(1)} %bitcast.129), kind=kOutput, calls=%fused_computation.13 | convolution fusion | flops 277082112 | bytes 8503808 | tf_op jit(solution)/shard_map/dot_general | solution.py:115
  241.6 6.5 %all-to-all-start = ((f32[32,1,768]{2,1,0:T(1,128)}), f32[32,1,768]{2,1,0:T(1,128)S(1)}, u32[]{:S(2)}, u32[]{:S(2)}) async-start(f32[32,1,768]{2,1,0:T(1,128)} %reshape.454), calls=%async_computation | async-start | bytes 196608 | tf_op jit(solution)/shard_map/all_to_all | solution.py:128
  248.1 2.6 slice_convert_fusion.1
  257.8 50.9 %all-gather = f32[48,2,2,64]{3,2,1,0:T(2,128)S(1)} all-gather(f32[3,2,2,64]{3,2,1,0:T(2,128)S(1)} %pad_maximum_fusion.1), channel_id=2, replica_groups=mesh['tm'=16,'space'=32] {'tm'}, dimensions={0}, use_global_device_ids=true | all-gather | bytes 52224 | tf_op jit(solution)/shard_map/all_gather | solution.py:130
  (119 shorter events, 30.4 us)
Async XLA Ops:
  7.2 1.7 copy-start
  7.2 146.3 %copy-start.4 = (bf16[8,64,256]{2,1,0:T(8,128)(2,1)S(1)}, bf16[8,64,256]{2,1,0:T(8,128)(2,1)}, u32[]{:S(2)}) copy-start(bf16[8,64,256]{2,1,0:T(8,128)(2,1)} %param.10) | copy-start | bytes 786436
  7.2 142.5 %all-gather.3.cloned.1.call-start = ((), (), s32[]{:S(2)}) async-start(), calls=%async_computation.1 | async-start | bytes 5406720 | tf_op jit(solution)/shard_map/all_gather | solution.py:68
  9.5 15.8 %collective-permute-start = (bf16[4,64,256]{2,1,0:T(8,128)(2,1)S(1)}, bf16[4,64,256]{2,1,0:T(8,128)(2,1)S(1)}, u32[]{:S(2)}, u32[]{:S(2)}) collective-permute-start(bf16[4,64,256]{2,1,0:T(8,128)(2,1)S(1)} %broadcast_select_fusion), channel_id=1, source_target_pairs={{0,32},{32,0},{64,96},{96,64},{128,160},{160,128},{192,224},{224,1... | collective-permute-start | bytes 393224 | tf_op jit(solution)/shard_map/ppermute | solution.py:18
  14.6 5.8 %collective-permute-start.4 = (bf16[2,64,64]{2,1,0:T(8,128)(2,1)S(1)}, bf16[2,64,64]{2,1,0:T(8,128)(2,1)S(1)}, u32[]{:S(2)}, u32[]{:S(2)}) collective-permute-start(bf16[2,64,64]{2,1,0:T(8,128)(2,1)S(1)} %broadcast_select_fusion.10), channel_id=1, source_target_pairs={{0,32},{32,0},{64,96},{96,64},{128,160},{160,128},{192,224},{224,1... | collective-permute-start | bytes 49160 | tf_op jit(solution)/shard_map/ppermute | solution.py:18
  20.5 7.5 %collective-permute-start.5 = (bf16[2,64,64]{2,1,0:T(8,128)(2,1)S(1)}, bf16[2,64,64]{2,1,0:T(8,128)(2,1)S(1)}, u32[]{:S(2)}, u32[]{:S(2)}) collective-permute-start(bf16[2,64,64]{2,1,0:T(8,128)(2,1)S(1)} %broadcast_select_fusion.11), channel_id=1, source_target_pairs={{0,64},{32,96},{64,0},{96,32},{128,192},{160,224},{192,128},{224,1... | collective-permute-start | bytes 49160 | tf_op jit(solution)/shard_map/ppermute | solution.py:18
  25.4 11.7 %collective-permute-start.1 = (bf16[4,64,256]{2,1,0:T(8,128)(2,1)S(1)}, bf16[4,64,256]{2,1,0:T(8,128)(2,1)S(1)}, u32[]{:S(2)}, u32[]{:S(2)}) collective-permute-start(bf16[4,64,256]{2,1,0:T(8,128)(2,1)S(1)} %broadcast_select_fusion.1), channel_id=1, source_target_pairs={{0,64},{32,96},{64,0},{96,32},{128,192},{160,224},{192,128},{224,1... | collective-permute-start | bytes 393224 | tf_op jit(solution)/shard_map/ppermute | solution.py:18
  28.1 14.9 %collective-permute-start.6 = (bf16[2,64,64]{2,1,0:T(8,128)(2,1)S(1)}, bf16[2,64,64]{2,1,0:T(8,128)(2,1)S(1)}, u32[]{:S(2)}, u32[]{:S(2)}) collective-permute-start(bf16[2,64,64]{2,1,0:T(8,128)(2,1)S(1)} %broadcast_select_fusion.12), channel_id=1, source_target_pairs={{0,128},{32,160},{64,192},{96,224},{128,0},{160,32},{192,64},{224,... | collective-permute-start | bytes 49160 | tf_op jit(solution)/shard_map/ppermute | solution.py:18
  37.2 17.3 %collective-permute-start.2 = (bf16[4,64,256]{2,1,0:T(8,128)(2,1)S(1)}, bf16[4,64,256]{2,1,0:T(8,128)(2,1)S(1)}, u32[]{:S(2)}, u32[]{:S(2)}) collective-permute-start(bf16[4,64,256]{2,1,0:T(8,128)(2,1)S(1)} %broadcast_select_fusion.2), channel_id=1, source_target_pairs={{0,128},{32,160},{64,192},{96,224},{128,0},{160,32},{192,64},{224,... | collective-permute-start | bytes 393224 | tf_op jit(solution)/shard_map/ppermute | solution.py:18
  43.1 25.6 %collective-permute-start.7 = (bf16[2,64,64]{2,1,0:T(8,128)(2,1)S(1)}, bf16[2,64,64]{2,1,0:T(8,128)(2,1)S(1)}, u32[]{:S(2)}, u32[]{:S(2)}) collective-permute-start(bf16[2,64,64]{2,1,0:T(8,128)(2,1)S(1)} %broadcast_select_fusion.13), channel_id=1, source_target_pairs={{0,256},{32,288},{64,320},{96,352},{128,384},{160,416},{192,448},{... | collective-permute-start | bytes 49160 | tf_op jit(solution)/shard_map/ppermute | solution.py:18
  54.6 25.5 %collective-permute-start.3 = (bf16[4,64,256]{2,1,0:T(8,128)(2,1)S(1)}, bf16[4,64,256]{2,1,0:T(8,128)(2,1)S(1)}, u32[]{:S(2)}, u32[]{:S(2)}) collective-permute-start(bf16[4,64,256]{2,1,0:T(8,128)(2,1)S(1)} %broadcast_select_fusion.3), channel_id=1, source_target_pairs={{0,256},{32,288},{64,320},{96,352},{128,384},{160,416},{192,448},{... | collective-permute-start | bytes 393224 | tf_op jit(solution)/shard_map/ppermute | solution.py:18
  82.6 7.2 %collective-permute-start.8 = (bf16[2,64,256]{2,1,0:T(8,128)(2,1)S(1)}, bf16[2,64,256]{2,1,0:T(8,128)(2,1)S(1)}, u32[]{:S(2)}, u32[]{:S(2)}) collective-permute-start(bf16[2,64,256]{2,1,0:T(8,128)(2,1)S(1)} %broadcast_select_fusion.5), channel_id=1, source_target_pairs={{0,32},{32,0},{64,96},{96,64},{128,160},{160,128},{192,224},{224,1... | collective-permute-start | bytes 196616 | tf_op jit(solution)/shard_map/ppermute | solution.py:18
  89.9 7.7 %collective-permute-start.9 = (bf16[2,64,256]{2,1,0:T(8,128)(2,1)S(1)}, bf16[2,64,256]{2,1,0:T(8,128)(2,1)S(1)}, u32[]{:S(2)}, u32[]{:S(2)}) collective-permute-start(bf16[2,64,256]{2,1,0:T(8,128)(2,1)S(1)} %broadcast_select_fusion.6), channel_id=1, source_target_pairs={{0,64},{32,96},{64,0},{96,32},{128,192},{160,224},{192,128},{224,1... | collective-permute-start | bytes 196616 | tf_op jit(solution)/shard_map/ppermute | solution.py:18
  97.6 11.5 %collective-permute-start.10 = (bf16[2,64,256]{2,1,0:T(8,128)(2,1)S(1)}, bf16[2,64,256]{2,1,0:T(8,128)(2,1)S(1)}, u32[]{:S(2)}, u32[]{:S(2)}) collective-permute-start(bf16[2,64,256]{2,1,0:T(8,128)(2,1)S(1)} %broadcast_select_fusion.7), channel_id=1, source_target_pairs={{0,128},{32,160},{64,192},{96,224},{128,0},{160,32},{192,64},{224,... | collective-permute-start | bytes 196616 | tf_op jit(solution)/shard_map/ppermute | solution.py:18
  109.2 16.4 %collective-permute-start.11 = (bf16[2,64,256]{2,1,0:T(8,128)(2,1)S(1)}, bf16[2,64,256]{2,1,0:T(8,128)(2,1)S(1)}, u32[]{:S(2)}, u32[]{:S(2)}) collective-permute-start(bf16[2,64,256]{2,1,0:T(8,128)(2,1)S(1)} %broadcast_select_fusion.8), channel_id=1, source_target_pairs={{0,256},{32,288},{64,320},{96,352},{128,384},{160,416},{192,448},{... | collective-permute-start | bytes 196616 | tf_op jit(solution)/shard_map/ppermute | solution.py:18
  155.3 4.0 %copy-start.1 = (f32[640,4096]{1,0:T(8,128)}, f32[640,4096]{1,0:T(8,128)S(1)}, u32[]{:S(2)}) copy-start(f32[640,4096]{1,0:T(8,128)S(1)} %get-tuple-element.71) | copy-start | bytes 31457284
  161.1 9.7 %slice-start = ((bf16[2,2048,578]{2,1,0:T(8,128)(2,1)}), bf16[2,2048,64]{2,1,0:T(8,128)(2,1)S(1)}, s32[]{:S(2)}) async-start(bf16[2,2048,578]{2,1,0:T(8,128)(2,1)} %all-gather.3.cloned.1.call-done), calls=%async_computation.2 | async-start | bytes 2097152 | tf_op jit(solution)/shard_map/slice | solution.py:74
  161.2 9.6 %copy-start.2 = (f32[640,4096]{1,0:T(8,128)S(1)}, f32[640,4096]{1,0:T(8,128)}, u32[]{:S(2)}) copy-start(f32[640,4096]{1,0:T(8,128)} %copy-done.1) | copy-start | bytes 31457284
  227.0 6.4 %copy-start.3 = (f32[4096,512]{0,1:T(8,128)S(1)}, f32[4096,512]{0,1:T(8,128)}, u32[]{:S(2)}) copy-start(f32[4096,512]{0,1:T(8,128)} %get-tuple-element.72) | copy-start | bytes 25165828
  241.6 14.4 %all-to-all-start = ((f32[32,1,768]{2,1,0:T(1,128)}), f32[32,1,768]{2,1,0:T(1,128)S(1)}, u32[]{:S(2)}, u32[]{:S(2)}) async-start(f32[32,1,768]{2,1,0:T(1,128)} %reshape.454), calls=%async_computation | async-start | bytes 196608 | tf_op jit(solution)/shard_map/all_to_all | solution.py:128
Sparse Core Ops, SparseCore 0:
  81.1 68.4 all-gather.2
where the time goes:
time: 317 us; the launch traced here: 316 us
  blocking collectives  94 us (30%)
  starting transfers between devices  74 us (23%)
  waiting for transfers between devices  59.7 us (19%)
  other arithmetic  30.3 us (10%)
  local copies, waits for them, and re-layouts  23.8 us (8%)
  matrix products  18.7 us (6%)
  between operations  15.8 us (5%)
    ppermute x12, starting transfers between devices, broadcast_tm(): received = lax.ppermute(values, axis, pairs)  67.4 us
    all_gather x1, blocking collectives, body(): joined = lax.all_gather(jnp.stack([m, t, n]), 'tm', axis=0, tiled=False)  50.9 us
    all_gather x1, blocking collectives, body(): lax.all_gather(part, 'space', axis=1, tiled=True)  43.1 us
    ppermute x12, waiting for transfers between devices, broadcast_tm(): received = lax.ppermute(values, axis, pairs)  35.7 us
    all_gather x1, waiting for transfers between devices, body(): gathered = lax.all_gather(packed, 'space', axis=1, tiled=True)  23.9 us
    reduce_sum x2, other arithmetic, body(): col_total = jnp.sum(expo, axis=0)  8.21 us
    dot_general x2, matrix products, body(): lax.dot_general(q, mem_keys[step], (((1,), (1,)), ((), ())), preferred_el...  7.93 us
    dot_general x2, matrix products, body(): picked = jnp.dot(readout, onehot_t, preferred_element_type=jnp.float32)  7.4 us
  transfers between devices with their start and end apart: 14, of which 7 were waited for; matrix products, arithmetic and copies ran while one was open for 6% of the time, Pallas kernels for 0%

commit v1 on v0

--- a/solution.py
+++ b/solution.py
@@ -120,9 +120,9 @@
         stats.append(jnp.stack([col_max, col_total, col_num]))
         if step + 1 < total_steps:
             part = out[rows:].reshape(keyframes, pix_dev, channels)
-            mem_values = lax.all_gather(part, "space", axis=1, tiled=True).reshape(
-                mem_width, channels
-            )
+            mem_values = jnp.concatenate(
+                lax.all_to_all(jnp.stack([part] * lax.axis_size("space")), "space", 0, 0), axis=1
+            ).reshape(mem_width, channels)
     local = jnp.stack(stats).reshape(total_steps, 3, keyframes, n_space, pix_dev)
     local = local.transpose(3, 1, 0, 2, 4)
     spread = lax.all_to_all(local, "space", 0, 0, tiled=True)

time: 317 us -> 284 us (0.90)
  blocking collectives: 94 us -> 51.9 us
  starting transfers between devices: 74 us -> 82.1 us
  other arithmetic: 30.3 us -> 23.9 us
    all_gather x1 -> x0, blocking collectives: 43.1 us -> none  [body(): lax.all_gather(part, 'space', axis=1, tiled=True)]
    all_to_all x0 -> x1, starting transfers between devices: none -> 6.89 us  [body(): lax.all_to_all(jnp.stack([part] * lax.axis_size('space')), 'space', 0, 0)]
    reduce_sum x1, other arithmetic: 6.14 us -> 2.01 us  [body(): total = jnp.sum(weights, axis=1, keepdims=True)]
    dot_general x2, matrix products: 3.41 us -> 6.88 us  [body(): jnp.dot(weights.astype(jnp.bfloat16), mem_values, preferred_element_type=...]
    unnamed x17 -> x21, local copies, waits for them, and re-layouts: 5.41 us -> 6.59 us
  transfers between devices with their start and end apart: 14 -> 15, of which waited for: 7 -> 8; matrix products, arithmetic and copies ran while one was open for 6% -> 11% of each run, Pallas kernels for 0% -> 0%
where the time goes in v1:
time: 284 us; the launch traced here: 283 us
  starting transfers between devices  82.1 us (29%)
  waiting for transfers between devices  62.2 us (22%)
  blocking collectives  51.9 us (18%)
  local copies, waits for them, and re-layouts  26.9 us (9%)
  other arithmetic  23.9 us (8%)
  matrix products  20.1 us (7%)
  between operations  15.9 us (6%)
    ppermute x12, starting transfers between devices, broadcast_tm(): received = lax.ppermute(values, axis, pairs)  67.4 us
    all_gather x1, blocking collectives, body(): joined = lax.all_gather(jnp.stack([m, t, n]), 'tm', axis=0, tiled=False)  51.9 us
    ppermute x12, waiting for transfers between devices, broadcast_tm(): received = lax.ppermute(values, axis, pairs)  35.7 us
    all_gather x1, waiting for transfers between devices, body(): gathered = lax.all_gather(packed, 'space', axis=1, tiled=True)  23.9 us
    dot_general x2, matrix products, body(): lax.dot_general(q, mem_keys[step], (((1,), (1,)), ((), ())), preferred_el...  7.88 us
    all_to_all x1, starting transfers between devices, body(): spread = lax.all_to_all(local, 'space', 0, 0, tiled=True)  7.72 us
    reduce_sum x2, other arithmetic, body(): col_total = jnp.sum(expo, axis=0)  7.65 us
    all_to_all x1, starting transfers between devices, body(): lax.all_to_all(jnp.stack([part] * lax.axis_size('space')), 'space', 0, 0)  6.89 us
  transfers between devices with their start and end apart: 15, of which 8 were waited for; matrix products, arithmetic and copies ran while one was open for 11% of the time, Pallas kernels for 0%

profile of v1, /device:TPU:2, one launch (start us, length us, event | category | flops | bytes accessed | tf_op | source)
XLA Modules:
  0.0 282.9 jit_solution(12721235568000709396)
XLA Ops:
  9.5 3.5 %collective-permute-start = (bf16[4,64,256]{2,1,0:T(8,128)(2,1)S(1)}, bf16[4,64,256]{2,1,0:T(8,128)(2,1)S(1)}, u32[]{:S(2)}, u32[]{:S(2)}) collective-permute-start(bf16[4,64,256]{2,1,0:T(8,128)(2,1)S(1)} %broadcast_select_fusion), channel_id=1, source_target_pairs={{0,32},{32,0},{64,96},{96,64},{128,160},{160,128},{192,224},{224,1... | collective-permute-start | bytes 393224 | tf_op jit(solution)/shard_map/ppermute | solution.py:18
  14.6 2.3 collective-permute-start.4
  20.5 4.8 %collective-permute-start.5 = (bf16[2,64,64]{2,1,0:T(8,128)(2,1)S(1)}, bf16[2,64,64]{2,1,0:T(8,128)(2,1)S(1)}, u32[]{:S(2)}, u32[]{:S(2)}) collective-permute-start(bf16[2,64,64]{2,1,0:T(8,128)(2,1)S(1)} %broadcast_select_fusion.11), channel_id=1, source_target_pairs={{0,64},{32,96},{64,0},{96,32},{128,192},{160,224},{192,128},{224,1... | collective-permute-start | bytes 49160 | tf_op jit(solution)/shard_map/ppermute | solution.py:18
  25.4 2.5 collective-permute-start.1
  28.1 9.1 %collective-permute-start.6 = (bf16[2,64,64]{2,1,0:T(8,128)(2,1)S(1)}, bf16[2,64,64]{2,1,0:T(8,128)(2,1)S(1)}, u32[]{:S(2)}, u32[]{:S(2)}) collective-permute-start(bf16[2,64,64]{2,1,0:T(8,128)(2,1)S(1)} %broadcast_select_fusion.12), channel_id=1, source_target_pairs={{0,128},{32,160},{64,192},{96,224},{128,0},{160,32},{192,64},{224,... | collective-permute-start | bytes 49160 | tf_op jit(solution)/shard_map/ppermute | solution.py:18
  37.2 5.7 %collective-permute-start.2 = (bf16[4,64,256]{2,1,0:T(8,128)(2,1)S(1)}, bf16[4,64,256]{2,1,0:T(8,128)(2,1)S(1)}, u32[]{:S(2)}, u32[]{:S(2)}) collective-permute-start(bf16[4,64,256]{2,1,0:T(8,128)(2,1)S(1)} %broadcast_select_fusion.2), channel_id=1, source_target_pairs={{0,128},{32,160},{64,192},{96,224},{128,0},{160,32},{192,64},{224,... | collective-permute-start | bytes 393224 | tf_op jit(solution)/shard_map/ppermute | solution.py:18
  43.1 10.9 %collective-permute-start.7 = (bf16[2,64,64]{2,1,0:T(8,128)(2,1)S(1)}, bf16[2,64,64]{2,1,0:T(8,128)(2,1)S(1)}, u32[]{:S(2)}, u32[]{:S(2)}) collective-permute-start(bf16[2,64,64]{2,1,0:T(8,128)(2,1)S(1)} %broadcast_select_fusion.13), channel_id=1, source_target_pairs={{0,256},{32,288},{64,320},{96,352},{128,384},{160,416},{192,448},{... | collective-permute-start | bytes 49160 | tf_op jit(solution)/shard_map/ppermute | solution.py:18
  54.6 14.0 %collective-permute-start.3 = (bf16[4,64,256]{2,1,0:T(8,128)(2,1)S(1)}, bf16[4,64,256]{2,1,0:T(8,128)(2,1)S(1)}, u32[]{:S(2)}, u32[]{:S(2)}) collective-permute-start(bf16[4,64,256]{2,1,0:T(8,128)(2,1)S(1)} %broadcast_select_fusion.3), channel_id=1, source_target_pairs={{0,256},{32,288},{64,320},{96,352},{128,384},{160,416},{192,448},{... | collective-permute-start | bytes 393224 | tf_op jit(solution)/shard_map/ppermute | solution.py:18
  68.8 11.4 %collective-permute-done.3 = bf16[4,64,256]{2,1,0:T(8,128)(2,1)S(1)} collective-permute-done((bf16[4,64,256]{2,1,0:T(8,128)(2,1)S(1)}, bf16[4,64,256]{2,1,0:T(8,128)(2,1)S(1)}, u32[]{:S(2)}, u32[]{:S(2)}) %collective-permute-start.3) | collective-permute-done | bytes 131104 | tf_op jit(solution)/shard_map/ppermute | solution.py:18
  82.6 2.1 collective-permute-start.8
  89.9 4.3 %collective-permute-start.9 = (bf16[2,64,256]{2,1,0:T(8,128)(2,1)S(1)}, bf16[2,64,256]{2,1,0:T(8,128)(2,1)S(1)}, u32[]{:S(2)}, u32[]{:S(2)}) collective-permute-start(bf16[2,64,256]{2,1,0:T(8,128)(2,1)S(1)} %broadcast_select_fusion.6), channel_id=1, source_target_pairs={{0,64},{32,96},{64,0},{96,32},{128,192},{160,224},{192,128},{224,1... | collective-permute-start | bytes 196616 | tf_op jit(solution)/shard_map/ppermute | solution.py:18
  94.3 3.3 %collective-permute-done.9 = bf16[2,64,256]{2,1,0:T(8,128)(2,1)S(1)} collective-permute-done((bf16[2,64,256]{2,1,0:T(8,128)(2,1)S(1)}, bf16[2,64,256]{2,1,0:T(8,128)(2,1)S(1)}, u32[]{:S(2)}, u32[]{:S(2)}) %collective-permute-start.9) | collective-permute-done | bytes 65568 | tf_op jit(solution)/shard_map/ppermute | solution.py:18
  97.6 1.9 collective-permute-start.10
  99.8 9.3 %collective-permute-done.10 = bf16[2,64,256]{2,1,0:T(8,128)(2,1)S(1)} collective-permute-done((bf16[2,64,256]{2,1,0:T(8,128)(2,1)S(1)}, bf16[2,64,256]{2,1,0:T(8,128)(2,1)S(1)}, u32[]{:S(2)}, u32[]{:S(2)}) %collective-permute-start.10) | collective-permute-done | bytes 65568 | tf_op jit(solution)/shard_map/ppermute | solution.py:18
  109.2 6.2 %collective-permute-start.11 = (bf16[2,64,256]{2,1,0:T(8,128)(2,1)S(1)}, bf16[2,64,256]{2,1,0:T(8,128)(2,1)S(1)}, u32[]{:S(2)}, u32[]{:S(2)}) collective-permute-start(bf16[2,64,256]{2,1,0:T(8,128)(2,1)S(1)} %broadcast_select_fusion.8), channel_id=1, source_target_pairs={{0,256},{32,288},{64,320},{96,352},{128,384},{160,416},{192,448},{... | collective-permute-start | bytes 196616 | tf_op jit(solution)/shard_map/ppermute | solution.py:18
  115.4 10.2 %collective-permute-done.11 = bf16[2,64,256]{2,1,0:T(8,128)(2,1)S(1)} collective-permute-done((bf16[2,64,256]{2,1,0:T(8,128)(2,1)S(1)}, bf16[2,64,256]{2,1,0:T(8,128)(2,1)S(1)}, u32[]{:S(2)}, u32[]{:S(2)}) %collective-permute-start.11) | collective-permute-done | bytes 65568 | tf_op jit(solution)/shard_map/ppermute | solution.py:18
  125.7 23.9 %all-gather.3.cloned.1.call-done = bf16[2,2048,578]{2,1,0:T(8,128)(2,1)} async-done(((bf16[2,64,578]{2,1,0:T(8,128)(2,1)}), bf16[2,2048,578]{2,1,0:T(8,128)(2,1)}) %all-gather.3.cloned.1.call-update) | async-done | bytes 4734992 | tf_op jit(solution)/shard_map/all_gather | solution.py:68
  149.7 3.8 %fusion.62 = (bf16[2,2048,256]{2,1,0:T(8,128)(2,1)}, bf16[2,2048,256]{2,1,0:T(8,128)(2,1)S(1)}) fusion(bf16[2,2048,578]{2,1,0:T(8,128)(2,1)} %all-gather.3.cloned.1.call-done), kind=kLoop, calls=%fused_computation.167 | loop fusion | bytes 8388608 | tf_op jit(solution)/shard_map/slice | solution.py:70
  153.5 1.8 select_reduce_fusion
  156.7 2.0 fusion.6
  158.7 2.0 fusion
  162.5 1.9 fusion.28
  164.4 2.7 multiply_reduce_fusion
  169.7 6.9 %all-to-all-start = ((bf16[32,2,4096]{2,1,0:T(2,128)(2,1)}), bf16[32,2,4096]{2,1,0:T(2,128)(2,1)S(1)}, u32[]{:S(2)}, u32[]{:S(2)}) async-start(bf16[32,2,4096]{2,1,0:T(2,128)(2,1)} %reshape.452), calls=%async_computation | async-start | bytes 1048576 | tf_op jit(solution)/shard_map/all_to_all | solution.py:124
  176.6 6.1 %select_reduce_fusion.1 = (f32[4096]{0:T(1024)S(1)}, f32[512]{0:T(512)S(1)}, f32[4096,512]{0,1:T(8,128)}) fusion(pred[512]{0:T(512)(128)(4,1)S(1)} %lt.168, pred[4096]{0:T(1024)(128)(4,1)S(1)} %lt.172, bf16[4096,256]{1,0:T(8,128)(2,1)} %bitcast.126, bf16[512,256]{1,0:T(8,128)(2,1)S(1)} %bitcast.143), kind=kOutput, calls=%fused_computation.15 | convolution fusion | flops 1084222976 | bytes 10770944 | tf_op jit(solution)/shard_map/dot_general | solution.py:99
  182.9 5.7 %fusion.5 = (f32[4096]{0:T(1024)S(1)}, f32[512]{0:T(512)S(1)}) fusion(f32[4096,512]{0,1:T(8,128)} %get-tuple-element.72, f32[4096]{0:T(1024)S(1)} %get-tuple-element.16, pred[512]{0:T(512)(128)(4,1)S(1)} %lt.168, f32[512]{0:T(512)S(1)} %get-tuple-element.17, pred[4096]{0:T(1024)(128)(4,1)S(1)} %lt.172), kind=kLoop, calls=%fused_computation.24 | loop fusion | flops 12578304 | bytes 8430080 | tf_op jit(solution)/shard_map/reduce_sum | solution.py:118
  188.7 2.5 slice_convert_fusion.1
  197.4 5.0 %fusion.19 = bf16[512,64]{0,1:T(8,128)(2,1)S(1)} fusion(bf16[4096,64]{0,1:T(8,128)(2,1)S(1)} %reshape_reshape.3, f32[4096,512]{0,1:T(8,128)} %get-tuple-element.72, f32[512]{0:T(512)S(1)} %get-tuple-element.17, pred[4096]{0:T(1024)(128)(4,1)S(1)} %lt.172, f32[512]{0:T(512)S(1)} %get-tuple-element.15, pred[512]{0:T(512)(128)(4,1)S(1)} %lt.168), kind=kOutput, calls=%fused_computation.37 | convolution fusion | flops 274825216 | bytes 8987136 | tf_op jit(solution)/shard_map/dot_general | solution.py:109
  203.3 2.6 fusion.2
  207.0 7.7 %all-to-all-start.1 = ((f32[32,1,768]{2,1,0:T(1,128)}), f32[32,1,768]{2,1,0:T(1,128)S(1)}, u32[]{:S(2)}, u32[]{:S(2)}) async-start(f32[32,1,768]{2,1,0:T(1,128)} %reshape.454), calls=%async_computation.1 | async-start | bytes 196608 | tf_op jit(solution)/shard_map/all_to_all | solution.py:128
  219.2 2.5 all-to-all-done.1
  223.4 51.9 %all-gather = f32[48,2,2,64]{3,2,1,0:T(2,128)S(1)} all-gather(f32[3,2,2,64]{3,2,1,0:T(2,128)S(1)} %pad_maximum_fusion.1), channel_id=2, replica_groups=mesh['tm'=16,'space'=32] {'tm'}, dimensions={0}, use_global_device_ids=true | all-gather | bytes 52224 | tf_op jit(solution)/shard_map/all_gather | solution.py:130
  (127 shorter events, 36.4 us)
Async XLA Ops:
  7.2 1.7 copy-start
  7.2 146.3 %copy-start.1 = (bf16[8,64,256]{2,1,0:T(8,128)(2,1)S(1)}, bf16[8,64,256]{2,1,0:T(8,128)(2,1)}, u32[]{:S(2)}) copy-start(bf16[8,64,256]{2,1,0:T(8,128)(2,1)} %param.10) | copy-start | bytes 786436
  7.2 142.5 %all-gather.3.cloned.1.call-start = ((), (), s32[]{:S(2)}) async-start(), calls=%async_computation.2 | async-start | bytes 5406720 | tf_op jit(solution)/shard_map/all_gather | solution.py:68
  9.5 15.8 %collective-permute-start = (bf16[4,64,256]{2,1,0:T(8,128)(2,1)S(1)}, bf16[4,64,256]{2,1,0:T(8,128)(2,1)S(1)}, u32[]{:S(2)}, u32[]{:S(2)}) collective-permute-start(bf16[4,64,256]{2,1,0:T(8,128)(2,1)S(1)} %broadcast_select_fusion), channel_id=1, source_target_pairs={{0,32},{32,0},{64,96},{96,64},{128,160},{160,128},{192,224},{224,1... | collective-permute-start | bytes 393224 | tf_op jit(solution)/shard_map/ppermute | solution.py:18
  14.6 5.8 %collective-permute-start.4 = (bf16[2,64,64]{2,1,0:T(8,128)(2,1)S(1)}, bf16[2,64,64]{2,1,0:T(8,128)(2,1)S(1)}, u32[]{:S(2)}, u32[]{:S(2)}) collective-permute-start(bf16[2,64,64]{2,1,0:T(8,128)(2,1)S(1)} %broadcast_select_fusion.10), channel_id=1, source_target_pairs={{0,32},{32,0},{64,96},{96,64},{128,160},{160,128},{192,224},{224,1... | collective-permute-start | bytes 49160 | tf_op jit(solution)/shard_map/ppermute | solution.py:18
  20.5 7.5 %collective-permute-start.5 = (bf16[2,64,64]{2,1,0:T(8,128)(2,1)S(1)}, bf16[2,64,64]{2,1,0:T(8,128)(2,1)S(1)}, u32[]{:S(2)}, u32[]{:S(2)}) collective-permute-start(bf16[2,64,64]{2,1,0:T(8,128)(2,1)S(1)} %broadcast_select_fusion.11), channel_id=1, source_target_pairs={{0,64},{32,96},{64,0},{96,32},{128,192},{160,224},{192,128},{224,1... | collective-permute-start | bytes 49160 | tf_op jit(solution)/shard_map/ppermute | solution.py:18
  25.4 11.7 %collective-permute-start.1 = (bf16[4,64,256]{2,1,0:T(8,128)(2,1)S(1)}, bf16[4,64,256]{2,1,0:T(8,128)(2,1)S(1)}, u32[]{:S(2)}, u32[]{:S(2)}) collective-permute-start(bf16[4,64,256]{2,1,0:T(8,128)(2,1)S(1)} %broadcast_select_fusion.1), channel_id=1, source_target_pairs={{0,64},{32,96},{64,0},{96,32},{128,192},{160,224},{192,128},{224,1... | collective-permute-start | bytes 393224 | tf_op jit(solution)/shard_map/ppermute | solution.py:18
  28.1 14.9 %collective-permute-start.6 = (bf16[2,64,64]{2,1,0:T(8,128)(2,1)S(1)}, bf16[2,64,64]{2,1,0:T(8,128)(2,1)S(1)}, u32[]{:S(2)}, u32[]{:S(2)}) collective-permute-start(bf16[2,64,64]{2,1,0:T(8,128)(2,1)S(1)} %broadcast_select_fusion.12), channel_id=1, source_target_pairs={{0,128},{32,160},{64,192},{96,224},{128,0},{160,32},{192,64},{224,... | collective-permute-start | bytes 49160 | tf_op jit(solution)/shard_map/ppermute | solution.py:18
  37.2 17.3 %collective-permute-start.2 = (bf16[4,64,256]{2,1,0:T(8,128)(2,1)S(1)}, bf16[4,64,256]{2,1,0:T(8,128)(2,1)S(1)}, u32[]{:S(2)}, u32[]{:S(2)}) collective-permute-start(bf16[4,64,256]{2,1,0:T(8,128)(2,1)S(1)} %broadcast_select_fusion.2), channel_id=1, source_target_pairs={{0,128},{32,160},{64,192},{96,224},{128,0},{160,32},{192,64},{224,... | collective-permute-start | bytes 393224 | tf_op jit(solution)/shard_map/ppermute | solution.py:18
  43.1 25.6 %collective-permute-start.7 = (bf16[2,64,64]{2,1,0:T(8,128)(2,1)S(1)}, bf16[2,64,64]{2,1,0:T(8,128)(2,1)S(1)}, u32[]{:S(2)}, u32[]{:S(2)}) collective-permute-start(bf16[2,64,64]{2,1,0:T(8,128)(2,1)S(1)} %broadcast_select_fusion.13), channel_id=1, source_target_pairs={{0,256},{32,288},{64,320},{96,352},{128,384},{160,416},{192,448},{... | collective-permute-start | bytes 49160 | tf_op jit(solution)/shard_map/ppermute | solution.py:18
  54.6 25.5 %collective-permute-start.3 = (bf16[4,64,256]{2,1,0:T(8,128)(2,1)S(1)}, bf16[4,64,256]{2,1,0:T(8,128)(2,1)S(1)}, u32[]{:S(2)}, u32[]{:S(2)}) collective-permute-start(bf16[4,64,256]{2,1,0:T(8,128)(2,1)S(1)} %broadcast_select_fusion.3), channel_id=1, source_target_pairs={{0,256},{32,288},{64,320},{96,352},{128,384},{160,416},{192,448},{... | collective-permute-start | bytes 393224 | tf_op jit(solution)/shard_map/ppermute | solution.py:18
  82.6 7.2 %collective-permute-start.8 = (bf16[2,64,256]{2,1,0:T(8,128)(2,1)S(1)}, bf16[2,64,256]{2,1,0:T(8,128)(2,1)S(1)}, u32[]{:S(2)}, u32[]{:S(2)}) collective-permute-start(bf16[2,64,256]{2,1,0:T(8,128)(2,1)S(1)} %broadcast_select_fusion.5), channel_id=1, source_target_pairs={{0,32},{32,0},{64,96},{96,64},{128,160},{160,128},{192,224},{224,1... | collective-permute-start | bytes 196616 | tf_op jit(solution)/shard_map/ppermute | solution.py:18
  89.9 7.7 %collective-permute-start.9 = (bf16[2,64,256]{2,1,0:T(8,128)(2,1)S(1)}, bf16[2,64,256]{2,1,0:T(8,128)(2,1)S(1)}, u32[]{:S(2)}, u32[]{:S(2)}) collective-permute-start(bf16[2,64,256]{2,1,0:T(8,128)(2,1)S(1)} %broadcast_select_fusion.6), channel_id=1, source_target_pairs={{0,64},{32,96},{64,0},{96,32},{128,192},{160,224},{192,128},{224,1... | collective-permute-start | bytes 196616 | tf_op jit(solution)/shard_map/ppermute | solution.py:18
  97.6 11.5 %collective-permute-start.10 = (bf16[2,64,256]{2,1,0:T(8,128)(2,1)S(1)}, bf16[2,64,256]{2,1,0:T(8,128)(2,1)S(1)}, u32[]{:S(2)}, u32[]{:S(2)}) collective-permute-start(bf16[2,64,256]{2,1,0:T(8,128)(2,1)S(1)} %broadcast_select_fusion.7), channel_id=1, source_target_pairs={{0,128},{32,160},{64,192},{96,224},{128,0},{160,32},{192,64},{224,... | collective-permute-start | bytes 196616 | tf_op jit(solution)/shard_map/ppermute | solution.py:18
  109.2 16.4 %collective-permute-start.11 = (bf16[2,64,256]{2,1,0:T(8,128)(2,1)S(1)}, bf16[2,64,256]{2,1,0:T(8,128)(2,1)S(1)}, u32[]{:S(2)}, u32[]{:S(2)}) collective-permute-start(bf16[2,64,256]{2,1,0:T(8,128)(2,1)S(1)} %broadcast_select_fusion.8), channel_id=1, source_target_pairs={{0,256},{32,288},{64,320},{96,352},{128,384},{160,416},{192,448},{... | collective-permute-start | bytes 196616 | tf_op jit(solution)/shard_map/ppermute | solution.py:18
  156.6 4.0 %slice-start = ((s8[5242880]{0:T(1024)(128)(4,1)}), s8[4194304]{0:T(1024)(128)(4,1)S(1)}, s32[]{:S(2)}) async-start(s8[5242880]{0:T(1024)(128)(4,1)} %bitcast.121), calls=%async_computation.3 | async-start | bytes 8388608
  158.7 3.8 %slice-start.2 = ((bf16[2,2048,578]{2,1,0:T(8,128)(2,1)}), bf16[2,2048,64]{2,1,0:T(8,128)(2,1)S(1)}, s32[]{:S(2)}) async-start(bf16[2,2048,578]{2,1,0:T(8,128)(2,1)} %all-gather.3.cloned.1.call-done), calls=%async_computation.5 | async-start | bytes 2097152 | tf_op jit(solution)/shard_map/slice | solution.py:74
  158.7 2.0 slice-start.1
  169.7 24.2 %all-to-all-start = ((bf16[32,2,4096]{2,1,0:T(2,128)(2,1)}), bf16[32,2,4096]{2,1,0:T(2,128)(2,1)S(1)}, u32[]{:S(2)}, u32[]{:S(2)}) async-start(bf16[32,2,4096]{2,1,0:T(2,128)(2,1)} %reshape.452), calls=%async_computation | async-start | bytes 1048576 | tf_op jit(solution)/shard_map/all_to_all | solution.py:124
  197.4 5.0 %slice-start.3 = ((s8[8388608]{0:T(1024)(128)(4,1)}), s8[4194304]{0:T(1024)(128)(4,1)S(1)}, s32[]{:S(2)}) async-start(s8[8388608]{0:T(1024)(128)(4,1)} %bitcast.124), calls=%async_computation.6 | async-start | bytes 8388608
  197.4 5.8 %slice-start.4 = ((s8[8388608]{0:T(1024)(128)(4,1)}), s8[4194304]{0:T(1024)(128)(4,1)S(1)}, s32[]{:S(2)}) async-start(s8[8388608]{0:T(1024)(128)(4,1)} %bitcast.124), calls=%async_computation.7 | async-start | bytes 8388608
  207.0 14.7 %all-to-all-start.1 = ((f32[32,1,768]{2,1,0:T(1,128)}), f32[32,1,768]{2,1,0:T(1,128)S(1)}, u32[]{:S(2)}, u32[]{:S(2)}) async-start(f32[32,1,768]{2,1,0:T(1,128)} %reshape.454), calls=%async_computation.1 | async-start | bytes 196608 | tf_op jit(solution)/shard_map/all_to_all | solution.py:128
Sparse Core Ops, SparseCore 0:
  81.1 68.4 all-gather.2
